TPU v7x, 512 devices: a whole 4x4x16 slice. The times are simulated.
512 devices in a mesh: dp: 16 (over z), row: 4 (over y), col: 8 (over x, core).
Axes of the slice: x: 4, y: 4, z: 16, core: 2. Of those that a mesh axis runs over, the one named last changes fastest.
Arguments:
- layer_input: bfloat16 [3072, 4096], P(('dp', 'col'), 'row'), may hold values from -6 to 6
- hidden_grad: bfloat16 [3072, 14336], P(('dp', 'row'), 'col'), may hold values from -6 to 6
- gate_slots: bfloat16 [4, 8, 48, 128, 128], P('row', 'col', 'dp'), may hold values from -0.125 to 0.125
- up_slots: bfloat16 [4, 8, 48, 128, 128], P('row', 'col', 'dp'), may hold values from -0.125 to 0.125
- block_mask: int32 [32, 112], replicated, may hold values from 0 to 1, as said below
Outputs:
- input_grad: bfloat16 [3072, 4096], P(('dp', 'col'), 'row')
- gate_slot_grad: float32 [4, 8, 48, 128, 128], P('row', 'col', 'dp')
- up_slot_grad: float32 [4, 8, 48, 128, 128], P('row', 'col', 'dp')
Inputs may be any that keep to these rules, and one draw needn't show every extreme that they name: `block_mask`: every tile of 8 x 14 blocks keeps between 24 and 48 blocks; some tile keeps exactly 48, which tile depends on the draw.
All inputs are finite; a program needn't handle non-finite values.
Results may differ from a plain program's by a relative error of at most 0.022.
Values may be sent and summed in bfloat16 or wider, within the bound.
No kernel may reach another device: no remote copies, remote signals or barrier semaphores. Data moves between devices by JAX's collectives and lax.ppermute only.
A program may use at most 64 MiB of HBM per device.

v0:
```python
import jax
import jax.numpy as jnp
from jax import lax
from jax.sharding import PartitionSpec as P


def slot_maps(block_mask, tile_rows, tile_cols, capacity):
    row_first = lax.axis_index("row") * tile_rows
    col_first = lax.axis_index("col") * tile_cols
    tile_mask = lax.dynamic_slice(block_mask, (row_first, col_first), (tile_rows, tile_cols))
    flat_mask = tile_mask.reshape(tile_rows * tile_cols)
    position = jnp.cumsum(flat_mask) - 1
    slot_ids = jnp.arange(capacity, dtype=jnp.int32)
    chosen = ((flat_mask[:, None] > 0) & (position[:, None] == slot_ids[None, :])).astype(jnp.int32)
    block_ids = jnp.arange(tile_rows * tile_cols, dtype=jnp.int32)
    slot_block = jnp.sum(chosen * block_ids[:, None], axis=0)
    live_slots = jnp.sum(chosen, axis=0).astype(jnp.float32)
    slot_row = slot_block // tile_cols
    slot_col = slot_block % tile_cols
    col_table = (slot_col[:, None] == jnp.arange(tile_cols, dtype=jnp.int32)[None, :]).astype(
        jnp.float32
    ) * live_slots[:, None]
    row_table = (slot_row[:, None] == jnp.arange(tile_rows, dtype=jnp.int32)[None, :]).astype(
        jnp.float32
    ) * live_slots[:, None]
    return (slot_row, slot_col, live_slots, col_table, row_table)


def slot_products(picked, pair_weights, col_table):
    per_slot = jnp.einsum("tsk,skn->tsn", picked, pair_weights, preferred_element_type=jnp.float32)
    return jnp.einsum("tsn,sc->tcn", per_slot, col_table, precision=lax.Precision.HIGHEST)


def back_products(grad_picked, pair_weights, row_table):
    per_slot = jnp.einsum(
        "tsn,skn->tsk", grad_picked, pair_weights, preferred_element_type=jnp.float32
    )
    return jnp.einsum("tsk,sr->trk", per_slot, row_table, precision=lax.Precision.HIGHEST)


def on_device(layer_input, hidden_grad, gate_slots, up_slots, block_mask):
    gate_local = gate_slots[0, 0]
    up_local = up_slots[0, 0]
    block_size = gate_local.shape[-1]
    replicas = lax.axis_size("dp")
    capacity = gate_local.shape[0] * replicas
    token_panel = lax.all_gather(layer_input, "col", axis=0, tiled=True)
    grad_panel = lax.all_gather(hidden_grad, "row", axis=0, tiled=True)
    tok_rows = token_panel.shape[0]
    feat_cols = token_panel.shape[1]
    unit_cols = grad_panel.shape[1]
    tile_rows = feat_cols // block_size
    tile_cols = unit_cols // block_size
    slot_row, slot_col, live_slots, col_table, row_table = slot_maps(
        block_mask, tile_rows, tile_cols, capacity
    )
    token_blocks = token_panel.reshape(tok_rows, tile_rows, block_size)
    picked_tokens = jnp.take(token_blocks, slot_row, axis=1)
    gate_all, up_all = (
        lax.all_gather(gate_local, "dp", axis=0, tiled=True),
        lax.all_gather(up_local, "dp", axis=0, tiled=True),
    )
    pair_all = jnp.concatenate([gate_all, up_all], axis=2)
    pair_part = slot_products(picked_tokens, pair_all, col_table)
    gate_part = pair_part[:, :, :block_size].reshape(tok_rows, unit_cols)
    up_part = pair_part[:, :, block_size:].reshape(tok_rows, unit_cols)
    gate_sum, up_sum = (
        lax.psum(gate_part.astype(jnp.bfloat16), "row").astype(jnp.float32),
        lax.psum(up_part.astype(jnp.bfloat16), "row").astype(jnp.float32),
    )
    sigmoid_gate = jax.nn.sigmoid(gate_sum)
    upstream = grad_panel.astype(jnp.float32)
    gate_grad = (upstream * up_sum * sigmoid_gate * (1.0 + gate_sum * (1.0 - sigmoid_gate))).astype(
        jnp.bfloat16
    )
    up_grad = (upstream * gate_sum * sigmoid_gate).astype(jnp.bfloat16)
    grad_pair = jnp.concatenate(
        [
            gate_grad.reshape(tok_rows, tile_cols, block_size),
            up_grad.reshape(tok_rows, tile_cols, block_size),
        ],
        axis=2,
    )
    grad_picked = jnp.take(grad_pair, slot_col, axis=1)
    summed = back_products(grad_picked, pair_all, row_table)
    input_sum = lax.psum_scatter(
        summed.reshape(tok_rows // lax.axis_size("col") * lax.axis_size("col"), feat_cols).astype(
            jnp.bfloat16
        ),
        "col",
        scatter_dimension=0,
        tiled=True,
    )
    pair_term = (
        jnp.einsum("tsk,tsn->skn", picked_tokens, grad_picked, preferred_element_type=jnp.float32)
        * live_slots[:, None, None]
    )
    pair_total = lax.psum_scatter(
        pair_term.astype(jnp.bfloat16), "dp", scatter_dimension=0, tiled=True
    ).astype(jnp.float32)
    gate_out = (pair_total[:, :, :block_size] / replicas)[None, None]
    up_out = (pair_total[:, :, block_size:] / replicas)[None, None]
    return (input_sum, gate_out, up_out)


def solution(mesh):
    return jax.shard_map(
        on_device,
        mesh=mesh,
        in_specs=(
            P(("dp", "col"), "row"),
            P(("dp", "row"), "col"),
            P("row", "col", "dp", None, None),
            P("row", "col", "dp", None, None),
            P(),
        ),
        out_specs=(
            P(("dp", "col"), "row"),
            P("row", "col", "dp", None, None),
            P("row", "col", "dp", None, None),
        ),
        check_vma=False,
    )
```

profile of v0, /device:TPU:8, one launch (start us, length us, event | category | flops | bytes accessed | tf_op | source)
XLA Modules:
  0.0 370.0 jit_solution(6575437389521833175)
XLA Ops:
  7.2 0.0 all-gather.5.cloned.1.call-start
  7.2 0.7 all-gather.5.cloned.1.call-update
  7.9 0.0 all-gather.7.cloned.1.call-start
  7.9 0.7 all-gather.7.cloned.1.call-update
  8.6 0.0 all-reduce.3.cloned.1.call-start
  8.7 0.8 broadcast_compare_fusion
  9.5 0.1 reshape.169
  9.6 0.2 reduce-window.8
  9.7 0.1 gt.16
  9.8 0.1 add_reduce_fusion
  9.9 0.1 convert_reduce_fusion
  10.1 13.5 %all_gather.15 = bf16[192,1024]{1,0:T(8,128)(2,1)S(1)} all-gather(bf16[24,1024]{1,0:T(8,128)(2,1)} %param.5), channel_id=1, replica_groups=mesh['dp'=16,'row'=4,'col'=8] {'col'}, dimensions={0}, use_global_device_ids=true | all-gather | bytes 442368 | tf_op jit(solution)/shard_map/all_gather | solution.py:47
  23.6 0.1 copy_bitcast_fusion.5
  23.7 1.0 gather_fusion
  24.7 0.0 copy-start
  24.7 61.7 %all-gather.5.cloned.1.call-done = bf16[1,1,48,128,128]{4,3,1,0,2:T(8,128)(2,1)} async-done(((bf16[1,1,3,128,128]{4,3,1,0,2:T(8,128)(2,1)}), bf16[1,1,48,128,128]{4,3,1,0,2:T(8,128)(2,1)}) %all-gather.5.cloned.1.call-update) | async-done | bytes 1572880 | tf_op jit(solution)/shard_map/all_gather | solution.py:60
  86.4 71.1 %all-gather.7.cloned.1.call-done = bf16[1,1,48,128,128]{4,3,1,0,2:T(8,128)(2,1)} async-done(((bf16[1,1,3,128,128]{4,3,1,0,2:T(8,128)(2,1)}), bf16[1,1,48,128,128]{4,3,1,0,2:T(8,128)(2,1)}) %all-gather.7.cloned.1.call-update) | async-done | bytes 1572880 | tf_op jit(solution)/shard_map/all_gather | solution.py:61
  157.5 3.3 convolution_bitcast_fusion
  160.8 0.0 copy-done
  160.8 9.9 %fusion.20 = bf16[192,14,256]{2,1,0:T(8,128)(2,1)S(1)} fusion(f32[192,48,256]{2,0,1:T(8,128)S(1)} %convolution_bitcast_fusion, f32[48]{0:T(128)S(1)} %convert_element_type.55, s32[48]{0:T(128)S(1)} %get-tuple-element.8), kind=kOutput, calls=%fused_computation.23 | convolution fusion | flops 397051200 | bytes 10813824 | tf_op jit(solution)/shard_map/tsn,sc->tcn/dot_general | solution.py:31
  170.7 0.3 fusion.60
  171.0 0.0 copy-start.3
  171.0 1.0 copy.56
  172.1 1.1 copy.57
  173.1 0.0 all-reduce.3.cloned.1.call-update
  173.2 0.0 reduce-scatter.5.cloned.1.call-start
  173.2 0.0 copy-done.3
  173.2 13.2 %all_gather.14 = bf16[192,1792]{1,0:T(8,128)(2,1)S(1)} all-gather(bf16[48,1792]{1,0:T(8,128)(2,1)S(1)} %copy-done.3), channel_id=1, replica_groups=mesh['dp'=16,'row'=4,'col'=8] {'row'}, dimensions={0}, use_global_device_ids=true | all-gather | bytes 860160 | tf_op jit(solution)/shard_map/all_gather | solution.py:48
  186.4 46.7 %all-reduce.3.cloned.1.call-done = (bf16[192,1792]{1,0:T(8,128)(2,1)}, bf16[192,1792]{1,0:T(8,128)(2,1)}) async-done(((bf16[192,1792]{1,0:T(8,128)(2,1)}, bf16[192,1792]{1,0:T(8,128)(2,1)}), (bf16[192,1792]{1,0:T(8,128)(2,1)}, bf16[192,1792]{1,0:T(8,128)(2,1)})) %all-reduce.3.cloned.1.call-update) | async-done | bytes 1376272 | tf_op jit(solution)/shard_map/psum | solution.py:68
  233.1 2.1 fusion.36
  235.1 0.2 copy.58
  235.3 0.2 copy.59
  235.5 0.2 pad_maximum_fusion.3
  235.7 3.1 gather_fusion.1
  238.8 6.2 %multiply_convert_fusion = bf16[48,128,256]{2,1,0:T(8,128)(2,1)} fusion(f32[48]{0:T(128)S(1)} %convert_element_type.55, bf16[48,192,256]{2,1,0:T(8,128)(2,1)} %gather_fusion.1, pred[48]{0:T(512)(128)(4,1)S(1)} %get-tuple-element.7, bf16[48,192,128]{2,1,0:T(8,128)(2,1)} %copy-done, pred[48]{0:T(512)(128)(4,1)S(1)} %get-tuple-element.22), kind=kOutput, calls=%fused_computation.4 | convolution fusion | flops 610664448 | bytes 10223904 | tf_op jit(solution)/shard_map/tsk,tsn->skn/dot_general | solution.py:95
  245.1 0.0 copy-start.1
  245.1 0.0 copy-start.2
  245.1 0.0 reduce-scatter.5.cloned.1.call-update
  245.1 0.0 reduce-scatter.3.cloned.1.call-start
  245.1 1.3 copy-done.1
  246.5 0.5 copy-done.2
  246.9 3.3 fusion.10
  250.3 4.9 %fusion.32 = bf16[8,192,128]{2,0,1:T(8,128)(2,1)S(1)} fusion(f32[192,48,128]{2,0,1:T(8,128)S(1)} %fusion.10, f32[48]{0:T(128)S(1)} %convert_element_type.55, s32[48]{0:T(128)S(1)} %get-tuple-element.23), kind=kOutput, calls=%fused_computation.34 | convolution fusion | flops 113443584 | bytes 5112192 | tf_op jit(solution)/shard_map/tsk,sr->trk/dot_general | solution.py:38
  255.2 0.8 copy.60
  256.0 0.0 reduce-scatter.3.cloned.1.call-update
  256.0 67.8 %reduce-scatter.5.cloned.1.call-done = bf16[3,128,256]{2,1,0:T(8,128)(2,1)} async-done(((bf16[48,128,256]{2,1,0:T(8,128)(2,1)}), bf16[3,128,256]{2,1,0:T(8,128)(2,1)}) %reduce-scatter.5.cloned.1.call-update) | async-done | bytes 196624 | tf_op jit(solution)/shard_map/reduce_scatter | solution.py:98
  323.8 1.0 convert_element_type.67
  324.8 0.8 fusion.37
  325.5 38.0 %reduce-scatter.3.cloned.1.call-done = bf16[24,1024]{1,0:T(8,128)(2,1)} async-done(((bf16[192,1024]{1,0:T(8,128)(2,1)}), bf16[24,1024]{1,0:T(8,128)(2,1)}) %reduce-scatter.3.cloned.1.call-update) | async-done | bytes 49168 | tf_op jit(solution)/shard_map/reduce_scatter | solution.py:86
  (4 shorter events, 0.1 us)
Async XLA Ops:
  7.2 79.3 %all-gather.5.cloned.1.call-start = ((), (), s32[]{:S(2)}) async-start(), calls=%async_computation.4 | async-start | bytes 1671168 | tf_op jit(solution)/shard_map/all_gather | solution.py:60
  7.9 149.6 %all-gather.7.cloned.1.call-start = ((), (), s32[]{:S(2)}) async-start(), calls=%async_computation.5 | async-start | bytes 1671168 | tf_op jit(solution)/shard_map/all_gather | solution.py:61
  8.6 224.4 %all-reduce.3.cloned.1.call-start = ((), (), s32[]{:S(2)}) async-start(), calls=%async_computation.6 | async-start | bytes 2752512 | tf_op jit(solution)/shard_map/psum | solution.py:68
  24.7 136.1 %copy-start = (bf16[48,192,128]{2,1,0:T(8,128)(2,1)}, bf16[48,192,128]{2,1,0:T(8,128)(2,1)S(1)}, u32[]{:S(2)}) copy-start(bf16[48,192,128]{2,1,0:T(8,128)(2,1)S(1)} %gather_fusion) | copy-start | bytes 7077892
  171.0 2.2 copy-start.3
  173.2 150.6 %reduce-scatter.5.cloned.1.call-start = ((), (), s32[]{:S(2)}) async-start(), calls=%async_computation.3 | async-start | bytes 3342336 | tf_op jit(solution)/shard_map/reduce_scatter | solution.py:98
  245.1 1.4 copy-start.1
  245.1 1.9 copy-start.2
  245.1 118.4 %reduce-scatter.3.cloned.1.call-start = ((), (), s32[]{:S(2)}) async-start(), calls=%async_computation.2 | async-start | bytes 442368 | tf_op jit(solution)/shard_map/reduce_scatter | solution.py:86
Sparse Core Ops, SparseCore 0:
  10.0 76.3 all-gather.4
  88.5 68.9 all-gather.6
  173.3 59.7 all-reduce.2
  245.2 78.5 reduce-scatter.4
  327.0 36.4 reduce-scatter.2
where the time goes:
time: 370 us
  waiting for transfers between devices  287 us (78%)
  matrix products  27.7 us (7%)
  blocking collectives  26.7 us (7%)
  between operations  13.9 us (4%)
  local copies, waits for them, and re-layouts  9.72 us (3%)
  other arithmetic  5.19 us (1%)
    all_gather x1, waiting for transfers between devices, on_device(): lax.all_gather(up_local, 'dp', axis=0, tiled=True)  71.1 us
    reduce_scatter x1, waiting for transfers between devices, on_device(): lax.psum_scatter(pair_term.astype(jnp.bfloat16), 'dp', scatter_dimension=...  67.8 us
    all_gather x1, waiting for transfers between devices, on_device(): lax.all_gather(gate_local, 'dp', axis=0, tiled=True)  61.7 us
    psum x1, waiting for transfers between devices, on_device(): lax.psum(gate_part.astype(jnp.bfloat16), 'row').astype(jnp.float32)  46.7 us
    reduce_scatter x1, waiting for transfers between devices, on_device(): lax.psum_scatter(summed.reshape(tok_rows // lax.axis_size('col') * lax.ax...  38 us
    all_gather x1, blocking collectives, on_device(): token_panel = lax.all_gather(layer_input, 'col', axis=0, tiled=True)  13.5 us
    all_gather x1, blocking collectives, on_device(): grad_panel = lax.all_gather(hidden_grad, 'row', axis=0, tiled=True)  13.2 us
    dot_general x1, matrix products, slot_products(): jnp.einsum('tsn,sc->tcn', per_slot, col_table, precision=lax.Precision.HI...  9.9 us
  transfers between devices with their start and end apart: 5, of which 5 were waited for; matrix products, arithmetic and copies ran while one was open for 4% of the time, Pallas kernels for 0%

commit v1 on v0

--- a/solution.py
+++ b/solution.py
@@ -44,7 +44,9 @@
     block_size = gate_local.shape[-1]
     replicas = lax.axis_size("dp")
     capacity = gate_local.shape[0] * replicas
-    token_panel = lax.all_gather(layer_input, "col", axis=0, tiled=True)
+    token_panel = jnp.concatenate(
+        lax.all_to_all(jnp.stack([layer_input] * lax.axis_size("col")), "col", 0, 0), axis=0
+    )
     grad_panel = lax.all_gather(hidden_grad, "row", axis=0, tiled=True)
     tok_rows = token_panel.shape[0]
     feat_cols = token_panel.shape[1]

time: 370 us -> 370 us (level)
  blocking collectives: 26.7 us -> 13.2 us
  waiting for transfers between devices: 287 us -> 294 us
  starting transfers between devices: 0.2 us -> 4.5 us
    all_gather x1 -> x0, blocking collectives: 13.5 us -> none  [on_device(): token_panel = lax.all_gather(layer_input, 'col', axis=0, tiled=True)]
    all_to_all x0 -> x1, waiting for transfers between devices: none -> 7.45 us  [on_device(): lax.all_to_all(jnp.stack([layer_input] * lax.axis_size('col')), 'col', 0, 0)]
    all_to_all x0 -> x1, starting transfers between devices: none -> 4.3 us  [on_device(): lax.all_to_all(jnp.stack([layer_input] * lax.axis_size('col')), 'col', 0, 0)]
  transfers between devices with their start and end apart: 5 -> 6, of which waited for: 5 -> 6; matrix products, arithmetic and copies ran while one was open for 4% -> 4% of each run, Pallas kernels for 0% -> 0%
where the time goes in v1:
time: 370 us
  waiting for transfers between devices  294 us (79%)
  matrix products  27.7 us (7%)
  between operations  13.9 us (4%)
  blocking collectives  13.2 us (4%)
  local copies, waits for them, and re-layouts  11.3 us (3%)
  other arithmetic  5.19 us (1%)
  starting transfers between devices  4.5 us (1%)
    all_gather x1, waiting for transfers between devices, on_device(): lax.all_gather(up_local, 'dp', axis=0, tiled=True)  71.1 us
    reduce_scatter x1, waiting for transfers between devices, on_device(): lax.psum_scatter(pair_term.astype(jnp.bfloat16), 'dp', scatter_dimension=...  67.9 us
    all_gather x1, waiting for transfers between devices, on_device(): lax.all_gather(gate_local, 'dp', axis=0, tiled=True)  61.8 us
    psum x1, waiting for transfers between devices, on_device(): lax.psum(gate_part.astype(jnp.bfloat16), 'row').astype(jnp.float32)  46.6 us
    reduce_scatter x1, waiting for transfers between devices, on_device(): lax.psum_scatter(summed.reshape(tok_rows // lax.axis_size('col') * lax.ax...  37.9 us
    all_gather x1, blocking collectives, on_device(): grad_panel = lax.all_gather(hidden_grad, 'row', axis=0, tiled=True)  13.2 us
    dot_general x1, matrix products, slot_products(): jnp.einsum('tsn,sc->tcn', per_slot, col_table, precision=lax.Precision.HI...  9.9 us
    all_to_all x1, waiting for transfers between devices, on_device(): lax.all_to_all(jnp.stack([layer_input] * lax.axis_size('col')), 'col', 0, 0)  7.45 us
  transfers between devices with their start and end apart: 6, of which 6 were waited for; matrix products, arithmetic and copies ran while one was open for 4% of the time, Pallas kernels for 0%

profile of v1, /device:TPU:8, one launch (start us, length us, event | category | flops | bytes accessed | tf_op | source)
XLA Modules:
  0.0 370.1 jit_solution(15470832604757055481)
XLA Ops:
  7.2 0.0 all-gather.5.cloned.1.call-start
  7.2 0.7 all-gather.5.cloned.1.call-update
  7.9 0.0 all-gather.7.cloned.1.call-start
  7.9 0.7 all-gather.7.cloned.1.call-update
  8.6 1.6 stack.2
  10.2 4.3 %all-to-all-start = ((bf16[8,24,1024]{2,1,0:T(8,128)(2,1)}), bf16[8,24,1024]{2,1,0:T(8,128)(2,1)S(1)}, u32[]{:S(2)}, u32[]{:S(2)}) async-start(bf16[8,24,1024]{2,1,0:T(8,128)(2,1)} %stack.2), calls=%async_computation | async-start | bytes 786432 | tf_op jit(solution)/shard_map/all_to_all | solution.py:48
  14.5 0.0 all-reduce.3.cloned.1.call-start
  14.6 0.8 broadcast_compare_fusion
  15.4 0.1 reshape.167
  15.4 0.2 reduce-window.8
  15.6 0.1 gt.16
  15.7 0.1 add_reduce_fusion
  15.8 0.1 convert_reduce_fusion
  16.0 7.4 %all-to-all-done = bf16[8,24,1024]{2,1,0:T(8,128)(2,1)S(1)} async-done(((bf16[8,24,1024]{2,1,0:T(8,128)(2,1)}), bf16[8,24,1024]{2,1,0:T(8,128)(2,1)S(1)}, u32[]{:S(2)}, u32[]{:S(2)}) %all-to-all-start) | async-done | bytes 393248 | tf_op jit(solution)/shard_map/all_to_all | solution.py:48
  23.4 0.1 copy.36
  23.5 0.1 copy.29
  23.6 1.0 gather_fusion
  24.6 0.0 copy-start
  24.6 61.8 %all-gather.5.cloned.1.call-done = bf16[1,1,48,128,128]{4,3,1,0,2:T(8,128)(2,1)} async-done(((bf16[1,1,3,128,128]{4,3,1,0,2:T(8,128)(2,1)}), bf16[1,1,48,128,128]{4,3,1,0,2:T(8,128)(2,1)}) %all-gather.5.cloned.1.call-update) | async-done | bytes 1572880 | tf_op jit(solution)/shard_map/all_gather | solution.py:62
  86.4 71.1 %all-gather.7.cloned.1.call-done = bf16[1,1,48,128,128]{4,3,1,0,2:T(8,128)(2,1)} async-done(((bf16[1,1,3,128,128]{4,3,1,0,2:T(8,128)(2,1)}), bf16[1,1,48,128,128]{4,3,1,0,2:T(8,128)(2,1)}) %all-gather.7.cloned.1.call-update) | async-done | bytes 1572880 | tf_op jit(solution)/shard_map/all_gather | solution.py:63
  157.5 3.3 convolution_bitcast_fusion
  160.8 0.0 copy-done
  160.8 9.9 %fusion.20 = bf16[192,14,256]{2,1,0:T(8,128)(2,1)S(1)} fusion(f32[192,48,256]{2,0,1:T(8,128)S(1)} %convolution_bitcast_fusion, f32[48]{0:T(128)S(1)} %convert_element_type.55, s32[48]{0:T(128)S(1)} %get-tuple-element.8), kind=kOutput, calls=%fused_computation.23 | convolution fusion | flops 397051200 | bytes 10813824 | tf_op jit(solution)/shard_map/tsn,sc->tcn/dot_general | solution.py:31
  170.7 0.3 fusion.60
  171.0 0.0 copy-start.3
  171.0 1.0 copy.55
  172.1 1.0 copy.56
  173.1 0.0 all-reduce.3.cloned.1.call-update
  173.1 0.0 reduce-scatter.5.cloned.1.call-start
  173.2 0.0 copy-done.3
  173.2 13.2 %all_gather.11 = bf16[192,1792]{1,0:T(8,128)(2,1)S(1)} all-gather(bf16[48,1792]{1,0:T(8,128)(2,1)S(1)} %copy-done.3), channel_id=1, replica_groups=mesh['dp'=16,'row'=4,'col'=8] {'row'}, dimensions={0}, use_global_device_ids=true | all-gather | bytes 860160 | tf_op jit(solution)/shard_map/all_gather | solution.py:50
  186.3 46.6 %all-reduce.3.cloned.1.call-done = (bf16[192,1792]{1,0:T(8,128)(2,1)}, bf16[192,1792]{1,0:T(8,128)(2,1)}) async-done(((bf16[192,1792]{1,0:T(8,128)(2,1)}, bf16[192,1792]{1,0:T(8,128)(2,1)}), (bf16[192,1792]{1,0:T(8,128)(2,1)}, bf16[192,1792]{1,0:T(8,128)(2,1)})) %all-reduce.3.cloned.1.call-update) | async-done | bytes 1376272 | tf_op jit(solution)/shard_map/psum | solution.py:70
  233.0 2.1 fusion.36
  235.1 0.2 copy.57
  235.2 0.2 copy.58
  235.4 0.2 pad_maximum_fusion.3
  235.6 3.1 gather_fusion.1
  238.8 6.3 %multiply_convert_fusion = bf16[48,128,256]{2,1,0:T(8,128)(2,1)} fusion(f32[48]{0:T(128)S(1)} %convert_element_type.55, bf16[48,192,256]{2,1,0:T(8,128)(2,1)} %gather_fusion.1, pred[48]{0:T(512)(128)(4,1)S(1)} %get-tuple-element.7, bf16[48,192,128]{2,1,0:T(8,128)(2,1)} %copy-done, pred[48]{0:T(512)(128)(4,1)S(1)} %get-tuple-element.22), kind=kOutput, calls=%fused_computation.4 | convolution fusion | flops 610664448 | bytes 10223904 | tf_op jit(solution)/shard_map/tsk,tsn->skn/dot_general | solution.py:97
  245.0 0.0 copy-start.1
  245.0 0.0 copy-start.2
  245.0 0.0 reduce-scatter.5.cloned.1.call-update
  245.0 0.0 reduce-scatter.3.cloned.1.call-start
  245.1 1.3 copy-done.1
  246.4 0.5 copy-done.2
  246.9 3.3 fusion.10
  250.2 4.9 %fusion.32 = bf16[8,192,128]{2,0,1:T(8,128)(2,1)S(1)} fusion(f32[192,48,128]{2,0,1:T(8,128)S(1)} %fusion.10, f32[48]{0:T(128)S(1)} %convert_element_type.55, s32[48]{0:T(128)S(1)} %get-tuple-element.23), kind=kOutput, calls=%fused_computation.34 | convolution fusion | flops 113443584 | bytes 5112192 | tf_op jit(solution)/shard_map/tsk,sr->trk/dot_general | solution.py:38
  255.1 0.8 copy.59
  256.0 0.0 reduce-scatter.3.cloned.1.call-update
  256.0 67.9 %reduce-scatter.5.cloned.1.call-done = bf16[3,128,256]{2,1,0:T(8,128)(2,1)} async-done(((bf16[48,128,256]{2,1,0:T(8,128)(2,1)}), bf16[3,128,256]{2,1,0:T(8,128)(2,1)}) %reduce-scatter.5.cloned.1.call-update) | async-done | bytes 196624 | tf_op jit(solution)/shard_map/reduce_scatter | solution.py:100
  323.9 1.0 convert_element_type.67
  324.9 0.8 fusion.37
  325.6 37.9 %reduce-scatter.3.cloned.1.call-done = bf16[24,1024]{1,0:T(8,128)(2,1)} async-done(((bf16[192,1024]{1,0:T(8,128)(2,1)}), bf16[24,1024]{1,0:T(8,128)(2,1)}) %reduce-scatter.3.cloned.1.call-update) | async-done | bytes 49168 | tf_op jit(solution)/shard_map/reduce_scatter | solution.py:88
  (4 shorter events, 0.1 us)
Async XLA Ops:
  7.2 79.3 %all-gather.5.cloned.1.call-start = ((), (), s32[]{:S(2)}) async-start(), calls=%async_computation.5 | async-start | bytes 1671168 | tf_op jit(solution)/shard_map/all_gather | solution.py:62
  7.9 149.6 %all-gather.7.cloned.1.call-start = ((), (), s32[]{:S(2)}) async-start(), calls=%async_computation.6 | async-start | bytes 1671168 | tf_op jit(solution)/shard_map/all_gather | solution.py:63
  10.2 13.2 %all-to-all-start = ((bf16[8,24,1024]{2,1,0:T(8,128)(2,1)}), bf16[8,24,1024]{2,1,0:T(8,128)(2,1)S(1)}, u32[]{:S(2)}, u32[]{:S(2)}) async-start(bf16[8,24,1024]{2,1,0:T(8,128)(2,1)} %stack.2), calls=%async_computation | async-start | bytes 786432 | tf_op jit(solution)/shard_map/all_to_all | solution.py:48
  14.5 218.5 %all-reduce.3.cloned.1.call-start = ((), (), s32[]{:S(2)}) async-start(), calls=%async_computation.7 | async-start | bytes 2752512 | tf_op jit(solution)/shard_map/psum | solution.py:70
  24.6 136.2 %copy-start = (bf16[48,192,128]{2,1,0:T(8,128)(2,1)}, bf16[48,192,128]{2,1,0:T(8,128)(2,1)S(1)}, u32[]{:S(2)}) copy-start(bf16[48,192,128]{2,1,0:T(8,128)(2,1)S(1)} %gather_fusion) | copy-start | bytes 7077892
  171.0 2.2 copy-start.3
  173.1 150.8 %reduce-scatter.5.cloned.1.call-start = ((), (), s32[]{:S(2)}) async-start(), calls=%async_computation.4 | async-start | bytes 3342336 | tf_op jit(solution)/shard_map/reduce_scatter | solution.py:100
  245.0 1.4 copy-start.1
  245.0 1.9 copy-start.2
  245.0 118.5 %reduce-scatter.3.cloned.1.call-start = ((), (), s32[]{:S(2)}) async-start(), calls=%async_computation.3 | async-start | bytes 442368 | tf_op jit(solution)/shard_map/reduce_scatter | solution.py:88
Sparse Core Ops, SparseCore 0:
  10.0 76.3 all-gather.4
  88.5 68.9 all-gather.6
  173.2 59.6 all-reduce.2
  245.2 78.6 reduce-scatter.4
  327.1 36.3 reduce-scatter.2
